TPU v7x, 128 devices: a whole 4x4x4 slice. The times are simulated.
128 devices in a mesh: req: 64 (over z, y, x), col: 2 (over core).
Axes of the slice: x: 4, y: 4, z: 4, core: 2. Of those that a mesh axis runs over, the one named last changes fastest.
Arguments:
- tokens: bfloat16 [32768, 1024], P(('req', 'col')), may hold values from -6 to 6
- norm_gain_pair: float32 [2, 1024], replicated, may hold values from 0.5 to 1.5
- query_key_value_weight: bfloat16 [3, 1024, 1024], P(None, None, 'col'), may hold values from -1 to 1
- head_gate_weight: bfloat16 [2, 1024, 8], P(None, None, 'col'), may hold values from -0.1875 to 0.1875
- decay_logit_bias: float32 [8], P('col'), may hold values from -1 to 1024, as said below
- adapter_down_factor: bfloat16 [64, 1024, 16], P('col'), may hold values from -0.1875 to 0.1875
- adapter_up_factor: bfloat16 [64, 16, 1024], P(None, None, 'col'), may hold values from -1.5 to 1.5
- lengths: int32 [64, 2, 3], P('req'), may hold values from 1 to 128, 256 in all within a row
- request_adapter_index: int32 [64, 6], P('req'), may hold values from 0 to 63
- request_cache_index: int32 [64, 6], P('req'), may hold values from 0 to 511
- caches: bfloat16 [256, 8, 128, 128], P('req', 'col'), may hold values from -6 to 6
- head_output_weight: bfloat16 [1024, 1024], P('col'), may hold values from -0.1875 to 0.1875
- feedforward_weight: bfloat16 [3, 1024, 2816], P(None, None, 'col'), may hold values from -0.1875 to 0.1875
Outputs:
- layer_out: bfloat16 [32768, 1024], P(('req', 'col'))
Inputs may be any that keep to these rules, and one draw needn't show every extreme that they name: The 3 lengths of one device sum to 256, and the longest of them is exactly 128. `request_cache_index`: a value of 256 or more means that the request has no cached memory state. `decay_logit_bias`: at most the logarithm of 512.
All inputs are finite; a program needn't handle non-finite values.
Results may differ from a plain program's by a relative error of at most 0.015.
Values may be sent and summed in bfloat16 or wider, within the bound.
No kernel may reach another device: no remote copies, remote signals or barrier semaphores. Data moves between devices by JAX's collectives and lax.ppermute only.
A program may use at most 192 MiB of HBM per device.

v0:
```python
import math
import jax
import jax.numpy as jnp
import numpy as np
from jax import lax
from jax.sharding import Mesh
from jax.sharding import PartitionSpec as P

epsilon = 1e-05
ROWS = ("z", "y", "x", "col")


def rms_scale(values, gain):
    widened = values.astype(jnp.float32)
    factor = lax.rsqrt(jnp.mean(widened * widened, axis=-1, keepdims=True) + epsilon)
    return (widened * factor * gain).astype(jnp.bfloat16)


def swap(value):
    return lax.ppermute(value, "col", perm=[(0, 1), (1, 0)])


def pair_rows(mine, other, col):
    first = jnp.where(col == 0, mine, other)
    second = jnp.where(col == 0, other, mine)
    return jnp.concatenate([first, second], axis=0)


def on_device(
    tokens,
    norm_gain_pair,
    query_key_value_weight,
    head_gate_weight,
    decay_logit_bias,
    adapter_down_factor,
    adapter_up_factor,
    lengths,
    request_adapter_index,
    request_cache_index,
    caches,
    head_output_weight,
    feedforward_weight,
):
    tok_rows, width = tokens.shape
    col = lax.axis_index("col")
    col_count = 2
    group = tok_rows * col_count
    head_cols = query_key_value_weight.shape[2]
    local_heads = head_gate_weight.shape[2]
    head_size = head_cols // local_heads
    group_lengths = lengths[0].reshape(-1)
    scale = 1.0 / math.sqrt(head_size)
    ff_other = swap(feedforward_weight)
    down_other = swap(adapter_down_factor)
    plane = lax.all_gather(caches, ("y", "x"), axis=0, tiled=True)
    per_plane = plane.shape[0]
    line_index = lax.all_gather(request_cache_index[0], "z", axis=0)
    local = line_index - lax.axis_index("z") * per_plane
    valid = (local >= 0) & (local < per_plane)
    picked = plane[jnp.clip(local, 0, per_plane - 1)]
    slots = jnp.where(valid[:, :, None, None, None], picked, jnp.zeros_like(picked))
    states = lax.psum_scatter(slots, "z", scatter_dimension=0, tiled=True)[0]
    normalized_rows = rms_scale(tokens, norm_gain_pair[0])
    gathered = pair_rows(normalized_rows, swap(normalized_rows), col)
    positions = jnp.arange(group, dtype=jnp.int32)
    ends = jnp.cumsum(group_lengths)
    starts = ends - group_lengths
    member = (
        (positions[:, None] >= starts[None, :]) & (positions[:, None] < ends[None, :])
    ).astype(jnp.float32)
    segment = jnp.sum((positions[:, None] >= ends[None, :]).astype(jnp.int32), axis=1)
    projected = jnp.einsum(
        "td,kdc->ktc", gathered, query_key_value_weight, preferred_element_type=jnp.float32
    )
    half_adapters = adapter_down_factor.shape[0]
    mine_numbers = col * half_adapters + jnp.arange(half_adapters, dtype=jnp.int32)
    other_numbers = (1 - col) * half_adapters + jnp.arange(half_adapters, dtype=jnp.int32)
    wanted = request_adapter_index[0][:, None]
    select_mine = (wanted == mine_numbers[None, :]).astype(jnp.bfloat16)
    select_other = (wanted == other_numbers[None, :]).astype(jnp.bfloat16)
    chosen = (
        jnp.einsum(
            "sa,adr->sdr", select_mine, adapter_down_factor, preferred_element_type=jnp.float32
        )
        + jnp.einsum("sa,adr->sdr", select_other, down_other, preferred_element_type=jnp.float32)
    ).astype(jnp.bfloat16)
    per_request = jnp.einsum("td,sdr->tsr", gathered, chosen, preferred_element_type=jnp.float32)
    low_rank_delta = jnp.sum(member[:, :, None] * per_request, axis=1)
    low_rank_delta = low_rank_delta.astype(jnp.bfloat16)
    adapter_onehot = (
        request_adapter_index[0][:, None]
        == jnp.arange(adapter_up_factor.shape[0], dtype=jnp.int32)[None, :]
    ).astype(jnp.bfloat16)
    up_chosen = jnp.einsum(
        "gq,qjl->gjl", adapter_onehot, adapter_up_factor, preferred_element_type=jnp.float32
    ).astype(jnp.bfloat16)
    delta_all = jnp.einsum(
        "tr,src->tsc", low_rank_delta, up_chosen, preferred_element_type=jnp.float32
    )
    delta = jnp.sum(member[:, :, None] * delta_all, axis=1)
    queries = (projected[0] + delta).astype(jnp.bfloat16).reshape(group, local_heads, head_size)
    keys = projected[1].astype(jnp.bfloat16).reshape(group, local_heads, head_size)
    values = projected[2].astype(jnp.bfloat16).reshape(group, local_heads, head_size)
    gate_terms = jnp.einsum(
        "td,kdh->kth", gathered, head_gate_weight, preferred_element_type=jnp.float32
    )
    log_keep = jax.nn.log_sigmoid(gate_terms[0] + decay_logit_bias[None, :])
    mix_gate = jax.nn.sigmoid(gate_terms[1])
    running = jnp.cumsum(log_keep, axis=0)
    before = running - log_keep
    start_hot = (positions[None, :] == starts[:, None]).astype(jnp.float32)
    start_level = jnp.sum(start_hot[:, :, None] * before[None, :, :], axis=1)
    level = running - jnp.sum(member[:, :, None] * start_level[None, :, :], axis=1)
    from_state = jnp.einsum("thi,shij->tshj", queries, states, preferred_element_type=jnp.float32)
    carried = jnp.sum(member[:, :, None, None] * from_state, axis=1) * jnp.exp(level)[:, :, None]
    scores = jnp.einsum("qhd,khd->hqk", queries, keys, preferred_element_type=jnp.float32) * scale
    allowed = (segment[:, None] == segment[None, :]) & (positions[None, :] <= positions[:, None])
    masked = jnp.where(allowed[None], scores, -jnp.inf)
    peak = jnp.max(masked, axis=2, keepdims=True)
    weights = jnp.exp(masked - peak)
    probs = (weights / jnp.sum(weights, axis=2, keepdims=True)).astype(jnp.bfloat16)
    attended = jnp.einsum("hqk,khd->qhd", probs, values, preferred_element_type=jnp.float32)
    gap = jnp.where(allowed[None], running.T[:, :, None] - running.T[:, None, :], -jnp.inf)
    memory_w = (scores * jnp.exp(gap)).astype(jnp.bfloat16)
    recalled = jnp.einsum("hqk,khd->qhd", memory_w, values, preferred_element_type=jnp.float32)
    recalled = recalled + carried
    factor = lax.rsqrt(jnp.mean(recalled * recalled, axis=2, keepdims=True) + epsilon)
    combined = attended + mix_gate[:, :, None] * recalled * factor
    head_out = combined.astype(jnp.bfloat16).reshape(group, head_cols)
    partial = jnp.dot(head_out, head_output_weight, preferred_element_type=jnp.float32)
    own = lax.dynamic_slice_in_dim(partial, col * tok_rows, tok_rows, axis=0)
    sent = lax.dynamic_slice_in_dim(partial, (1 - col) * tok_rows, tok_rows, axis=0)
    attn_proj = own + swap(sent)
    mixed = (tokens.astype(jnp.float32) + attn_proj).astype(jnp.bfloat16)
    normed_two = rms_scale(mixed, norm_gain_pair[1])

    def feed_half(weight):
        gate_up = jnp.einsum(
            "td,kdf->ktf", normed_two, weight[:2], preferred_element_type=jnp.float32
        )
        hidden = (jax.nn.silu(gate_up[0]) * gate_up[1]).astype(jnp.bfloat16)
        return jnp.einsum("tf,df->td", hidden, weight[2], preferred_element_type=jnp.float32)

    feed = feed_half(feedforward_weight) + feed_half(ff_other)
    return (mixed.astype(jnp.float32) + feed).astype(jnp.bfloat16)


def solution(mesh):
    n_req = mesh.shape["req"]
    side = round(n_req ** (1.0 / 3.0))
    devices = np.asarray(mesh.devices).reshape(
        side, side, n_req // (side * side), mesh.shape["col"]
    )
    grid = Mesh(devices, ROWS)
    placed = (
        P(ROWS, None),
        P(),
        P(None, None, "col"),
        P(None, None, "col"),
        P("col"),
        P("col", None, None),
        P(None, None, "col"),
        P(ROWS[:3], None, None),
        P(ROWS[:3], None),
        P(ROWS[:3], None),
        P(ROWS[:3], "col", None, None),
        P("col", None),
        P(None, None, "col"),
    )
    return jax.shard_map(
        on_device, mesh=grid, in_specs=placed, out_specs=P(ROWS, None), check_vma=False
    )
```

profile of v0, /device:TPU:1, one launch (start us, length us, event | category | flops | bytes accessed | tf_op | source)
XLA Modules:
  0.0 177.2 jit_solution(17302642569815768344)
XLA Ops:
  7.3 10.1 %all-gather = s32[4,1,6]{2,1,0:T(1,128)S(1)} all-gather(s32[1,1,6]{2,1,0:T(1,128)} %bitcast.159), channel_id=1, replica_groups=mesh['z'=4,'y'=4,'x'=4,'col'=2] {'z'}, dimensions={0}, use_global_device_ids=true | all-gather | bytes 120 | tf_op jit(solution)/shard_map/all_gather | solution.py:57
  17.5 1.2 fusion.33
  18.7 1.4 fusion.95
  20.1 63.2 %all-gather.3.cloned.1.call-done = bf16[64,4,128,128]{3,2,1,0:T(8,128)(2,1)} async-done(((bf16[4,4,128,128]{3,2,1,0:T(8,128)(2,1)}), bf16[64,4,128,128]{3,2,1,0:T(8,128)(2,1)}) %all-gather.3.cloned.1.call-update) | async-done | bytes 8388624 | tf_op jit(solution)/shard_map/all_gather | solution.py:55
  83.4 6.2 %gather_fusion = bf16[24,4,128,128]{3,2,1,0:T(8,128)(2,1)} fusion(bf16[64,4,128,128]{3,2,1,0:T(8,128)(2,1)} %all-gather.3.cloned.1.call-done, s32[1024]{0:T(1024)S(1)} %pad_clamp_fusion), kind=kCustom, calls=%fused_computation | custom fusion | bytes 6291552 | tf_op jit(solution)/shard_map/gather | solution.py:60
  89.5 4.7 %copy.59 = bf16[4,6,4,128,128]{3,4,1,2,0:T(8,128)(2,1)} copy(bf16[4,6,4,128,128]{4,3,2,1,0:T(8,128)(2,1)} %bitcast.136) | data formatting | bytes 6291456 | tf_op jit(solution)/shard_map/gather | solution.py:60
  94.3 3.8 %broadcast_select_fusion = bf16[4,6,4,128,128]{3,4,1,2,0:T(8,128)(2,1)} fusion(bf16[4,6,4,128,128]{3,4,1,2,0:T(8,128)(2,1)} %copy.59, pred[4,6]{1,0:T(4,128)(4,1)S(1)} %bitcast.156), kind=kLoop, calls=%fused_computation.16 | loop fusion | flops 1572864 | bytes 6291480 | tf_op jit(solution)/shard_map/jit(_where)/select_n | solution.py:61
  98.1 2.0 %fusion.35 = bf16[256,1024]{1,0:T(8,128)(2,1)} fusion(bf16[256,1024]{1,0:T(8,128)(2,1)} %param.13, f32[1024]{0:T(1024)S(1)} %bitcast.146, f32[256]{0:T(256)S(1)} %add_rsqrt_fusion.2), kind=kLoop, calls=%fused_computation.52 | loop fusion | flops 1048576 | bytes 1053696 | tf_op jit(solution)/shard_map/convert_element_type | solution.py:16
  100.9 2.8 %copy.49 = bf16[32,1024,16]{1,0,2:T(8,128)(2,1)} copy(bf16[32,1024,16]{1,2,0:T(8,128)(2,1)} %param.18) | data formatting | bytes 2097152 | tf_op args[5]
  106.5 2.7 %convolution_convert_fusion = bf16[6,16,512]{2,0,1:T(8,128)(2,1)S(1)} fusion(bf16[64,16,512]{2,1,0:T(8,128)(2,1)} %param.19, s32[6]{0:T(128)} %bitcast.151), kind=kOutput, calls=%fused_computation.48 | convolution fusion | flops 6340992 | bytes 1146904 | tf_op jit(solution)/shard_map/gq,qjl->gjl/dot_general | solution.py:94
  109.3 3.2 %fusion.73 = f32[6,1024,16]{1,0,2:T(8,128)} fusion(s32[32]{0:T(128)} %iota_add_fusion.1, s32[6]{0:T(128)} %bitcast.152, bf16[32,1024,16]{1,2,0:T(8,128)(2,1)} %param.18), kind=kOutput, calls=%fused_computation.111 | convolution fusion | flops 6291648 | bytes 1441944 | tf_op jit(solution)/shard_map/sa,adr->sdr/dot_general | solution.py:82
  112.5 1.6 broadcast_select_fusion.2
  114.9 1.1 convolution_bitcast_fusion.1
  117.3 1.3 reshape.277
  118.6 3.0 %reduce-window.18 = f32[4,4,128]{2,1,0:T(4,128)} reduce-window(f32[4,4,128]{2,1,0:T(4,128)} %reshape.277, f32[]{:T(128)} %constant.20.clone.1), window={size=1x1x128 pad=0_0x0_0x127_0}, to_apply=%region_7.8 | reduce-window | flops 260096 | bytes 16388 | tf_op jit(solution)/shard_map/reduce-window.1
  121.6 1.4 slice_reduce_fusion
  123.0 1.3 reduce-window.19
  125.2 3.1 %fusion.96 = (bf16[3,512,512]{1,2,0:T(8,128)(2,1)S(1)}, f32[3,512,512]{1,2,0:T(8,128)S(1)}) fusion(bf16[3,1024,512]{2,1,0:T(8,128)(2,1)S(1)} %copy-done, bf16[256,1024]{1,0:T(8,128)(2,1)} %copy-done.7, bf16[256,1024]{1,0:T(8,128)(2,1)} %copy-done.5), kind=kOutput, calls=%fused_computation.141 | convolution fusion | flops 1613496320 | bytes 8912896 | tf_op jit(solution)/shard_map/td,kdc->ktc/dot_general | solution.py:72
  130.5 1.1 fusion.94
  131.6 1.6 fusion.32
  133.8 1.0 multiply_reduce_fusion
  135.4 4.7 %fusion.97 = (f32[4,512]{1,0:T(4,128)S(1)}, f32[4,512,512]{1,2,0:T(8,128)}) fusion(pred[512,512]{0,1:T(8,128)(4,1)S(1)} %fusion.43, bf16[512,4,128]{0,2,1:T(8,128)(2,1)S(1)} %add_convert_fusion, bf16[512,4,128]{0,2,1:T(8,128)(2,1)} %bitcast.142), kind=kOutput, calls=%fused_computation.142 | convolution fusion | flops 272630272 | bytes 5513216 | tf_op jit(solution)/shard_map/sub | solution.py:120
  140.1 2.2 %fusion.1 = f32[512,4,128]{0,2,1:T(8,128)S(1)} fusion(f32[512,6]{0,1:T(8,128)S(1)} %fusion.60, bf16[1,6,4,128,128]{3,4,1,2,0:T(8,128)(2,1)} %reduce-scatter.2.cloned.1.call-done, bf16[512,4,128]{0,2,1:T(8,128)(2,1)S(1)} %add_convert_fusion), kind=kOutput, calls=%fused_computation.3 | convolution fusion | flops 405536768 | bytes 2371584 | tf_op jit(solution)/shard_map/thi,shij->tshj/dot_general | solution.py:114
  142.4 2.9 %multiply_reduce_fusion.1 = (f32[512,4]{0,1:T(4,128)S(1)}, f32[512,4,128]{0,2,1:T(8,128)}) fusion(f32[512,4,128]{0,2,1:T(8,128)S(1)} %fusion.1, f32[512,4]{0,1:T(4,128)S(1)} %copy-done.16, bf16[512,4,128]{0,2,1:T(8,128)(2,1)S(1)} %bitcast.140, f32[4,512]{1,0:T(4,128)S(1)} %bitcast.149, pred[512,512]{0,1:T(8,128)(4,1)S(1)} %fusion.43, ...), kind=kOutput, calls=%fused_computation.61 | convolution fusion | flops 543160320 | bytes 3956736 | tf_op jit(solution)/shard_map/hqk,khd->qhd/dot_general | solution.py:125
  145.3 3.1 %fusion.30 = bf16[512,4,128]{0,2,1:T(8,128)(2,1)S(1)} fusion(bf16[512,4,128]{0,2,1:T(8,128)(2,1)S(1)} %bitcast.141, f32[4,512,512]{1,2,0:T(8,128)} %get-tuple-element.16, f32[4,512]{1,0:T(4,128)S(1)} %get-tuple-element.15, f32[512,4,128]{0,2,1:T(8,128)} %get-tuple-element.18, f32[512,4]{0,1:T(4,128)S(1)} %add_rsqrt_fusion, f32[512,4]{0,1:T(4,128)S(1)} %copy-done.17), kind=kOutput, calls=%fused_computation.44 | convolution fusion | flops 271581184 | bytes 6316032 | tf_op jit(solution)/shard_map/hqk,khd->qhd/dot_general | solution.py:122
  149.2 1.2 constant_dynamic-slice_fusion
  150.4 3.0 %collective-permute-done.2 = f32[256,1024]{1,0:T(8,128)} collective-permute-done((f32[256,1024]{1,0:T(8,128)}, f32[256,1024]{1,0:T(8,128)}, u32[]{:S(2)}, u32[]{:S(2)}) %collective-permute-start.2) | collective-permute-done | bytes 1048608 | tf_op jit(solution)/shard_map/ppermute | solution.py:20
  153.4 1.5 fusion.37
  154.9 4.4 %fusion.6 = f32[2,256,1408]{2,1,0:T(8,128)S(1)} fusion(bf16[3,1024,1408]{2,1,0:T(8,128)(2,1)} %param.25, bf16[256,1024]{1,0:T(8,128)(2,1)S(1)} %get-tuple-element.6, f32[1024]{0:T(1024)S(1)} %bitcast.154, f32[256]{0:T(256)S(1)} %add_rsqrt_fusion.1), kind=kOutput, calls=%fused_computation.13 | convolution fusion | flops 1477443584 | bytes 9180160 | tf_op jit(solution)/shard_map/td,kdf->ktf/dot_general | solution.py:138
  159.3 2.9 %fusion.14 = f32[256,1024]{1,0:T(8,128)S(1)} fusion(bf16[3,1024,1408]{2,1,0:T(8,128)(2,1)} %param.25, f32[2,256,1408]{2,1,0:T(8,128)S(1)} %fusion.6), kind=kOutput, calls=%fused_computation.19 | convolution fusion | flops 740360192 | bytes 6815744 | tf_op jit(solution)/shard_map/tf,df->td/dot_general | solution.py:142
  162.2 4.4 %fusion.9 = f32[2,256,1408]{2,1,0:T(8,128)S(1)} fusion(bf16[3,1024,1408]{2,1,0:T(8,128)(2,1)} %collective-permute-done.3, bf16[256,1024]{1,0:T(8,128)(2,1)S(1)} %get-tuple-element.6, f32[1024]{0:T(1024)S(1)} %bitcast.155, f32[256]{0:T(256)S(1)} %add_rsqrt_fusion.1), kind=kOutput, calls=%fused_computation.14 | convolution fusion | flops 1477443584 | bytes 9180160 | tf_op jit(solution)/shard_map/td,kdf->ktf/dot_general | solution.py:138
  166.5 3.8 %fusion.31 = bf16[256,1024]{1,0:T(8,128)(2,1)} fusion(f32[256,1024]{1,0:T(8,128)S(1)} %fusion.14, bf16[3,1024,1408]{2,1,0:T(8,128)(2,1)} %collective-permute-done.3, bf16[256,1024]{1,0:T(8,128)(2,1)S(1)} %get-tuple-element.6, f32[2,256,1408]{2,1,0:T(8,128)S(1)} %fusion.9), kind=kOutput, calls=%fused_computation.45 | convolution fusion | flops 741408768 | bytes 7864320 | tf_op jit(solution)/shard_map/tf,df->td/dot_general | solution.py:142
  (96 shorter events, 11.5 us)
Async XLA Ops:
  6.5 118.6 %copy-start = (bf16[3,1024,512]{2,1,0:T(8,128)(2,1)S(1)}, bf16[3,1024,512]{2,1,0:T(8,128)(2,1)}, u32[]{:S(2)}) copy-start(bf16[3,1024,512]{2,1,0:T(8,128)(2,1)} %param.15) | copy-start | bytes 9437188
  6.5 76.8 %all-gather.3.cloned.1.call-start = ((), (), s32[]{:S(2)}) async-start(), calls=%async_computation.1 | async-start | bytes 8912896 | tf_op jit(solution)/shard_map/all_gather | solution.py:55
  7.3 132.8 %reduce-scatter.2.cloned.1.call-start = ((), (), s32[]{:S(2)}) async-start(), calls=%async_computation.2 | async-start | bytes 3932160 | tf_op jit(solution)/shard_map/reduce_scatter | solution.py:62
  20.1 78.0 %copy-start.12 = (f32[1,1024]{1,0:T(1,128)}, f32[1,1024]{1,0:T(1,128)S(1)}, u32[]{:S(2)}) copy-start(f32[1,1024]{1,0:T(1,128)S(1)} %get-tuple-element.12) | copy-start | bytes 12292
  98.1 6.0 %copy-start.24 = (s32[1,2,3]{2,1,0:T(2,128)S(1)}, s32[1,2,3]{2,1,0:T(2,128)}, u32[]{:S(2)}) copy-start(s32[1,2,3]{2,1,0:T(2,128)} %param.20) | copy-start | bytes 76
  98.1 2.0 %copy-start.15 = (f32[256]{0:T(256)}, f32[256]{0:T(256)S(1)}, u32[]{:S(2)}) copy-start(f32[256]{0:T(256)S(1)} %add_rsqrt_fusion.2) | copy-start | bytes 3076
  100.2 12.4 %collective-permute-start = (bf16[256,1024]{1,0:T(8,128)(2,1)}, bf16[256,1024]{1,0:T(8,128)(2,1)}, u32[]{:S(2)}, u32[]{:S(2)}) collective-permute-start(bf16[256,1024]{1,0:T(8,128)(2,1)} %fusion.35), channel_id=1, source_target_pairs={{0,1},{1,0},{2,3},{3,2},{4,5},{5,4},{6,7},{7,6},{8,9},{9,8},{10,11... | collective-permute-start | bytes 1572872 | tf_op jit(solution)/shard_map/ppermute | solution.py:20
  103.6 27.9 %collective-permute-start.1 = (bf16[32,1024,16]{1,0,2:T(8,128)(2,1)}, bf16[32,1024,16]{1,0,2:T(8,128)(2,1)}, u32[]{:S(2)}, u32[]{:S(2)}) collective-permute-start(bf16[32,1024,16]{1,0,2:T(8,128)(2,1)} %copy.49), channel_id=1, source_target_pairs={{0,1},{1,0},{2,3},{3,2},{4,5},{5,4},{6,7},{7,6},{8,9},{9,8},{10,11... | collective-permute-start | bytes 3145736 | tf_op jit(solution)/shard_map/ppermute | solution.py:20
  103.6 58.5 %collective-permute-start.3 = (bf16[3,1024,1408]{2,1,0:T(8,128)(2,1)}, bf16[3,1024,1408]{2,1,0:T(8,128)(2,1)}, u32[]{:S(2)}, u32[]{:S(2)}) collective-permute-start(bf16[3,1024,1408]{2,1,0:T(8,128)(2,1)} %param.25), channel_id=1, source_target_pairs={{0,1},{1,0},{2,3},{3,2},{4,5},{5,4},{6,7},{7,6},{8,9},{9,8},{10,11... | collective-permute-start | bytes 25952264 | tf_op jit(solution)/shard_map/ppermute | solution.py:20
  106.5 10.1 %copy-start.21 = (f32[4]{0:T(128)S(1)}, f32[4]{0:T(128)}, u32[]{:S(2)}) copy-start(f32[4]{0:T(128)} %param.17) | copy-start | bytes 52
  114.1 0.8 copy-start.5
  114.1 1.9 %copy-start.7 = (bf16[256,1024]{1,0:T(8,128)(2,1)}, bf16[256,1024]{1,0:T(8,128)(2,1)S(1)}, u32[]{:S(2)}) copy-start(bf16[256,1024]{1,0:T(8,128)(2,1)S(1)} %get-tuple-element.10) | copy-start | bytes 1572868
  116.0 0.6 copy-start.13
  125.1 3.1 %copy-start.14 = (f32[2,512,4]{1,2,0:T(4,128)S(1)}, f32[2,512,4]{1,2,0:T(4,128)}, u32[]{:S(2)}) copy-start(f32[2,512,4]{1,2,0:T(4,128)} %copy-done.13) | copy-start | bytes 49156
  125.1 3.1 %copy-start.22 = (f32[4]{0:T(128)S(1)}, f32[4]{0:T(128)}, u32[]{:S(2)}) copy-start(f32[4]{0:T(128)} %param.17) | copy-start | bytes 52
  125.1 3.9 %copy-start.11 = (f32[6,512]{1,0:T(8,128)S(1)}, f32[6,512]{1,0:T(8,128)}, u32[]{:S(2)}) copy-start(f32[6,512]{1,0:T(8,128)} %fusion.61) | copy-start | bytes 36868
  128.3 3.3 %copy-start.3 = (f32[6,1024,16]{1,0,2:T(8,128)S(1)}, f32[6,1024,16]{1,0,2:T(8,128)}, u32[]{:S(2)}) copy-start(f32[6,1024,16]{1,0,2:T(8,128)} %fusion.73) | copy-start | bytes 1179652
  128.3 3.3 %copy-start.19 = (s32[1,6]{1,0:T(1,128)S(1)}, s32[1,6]{1,0:T(1,128)}, u32[]{:S(2)}) copy-start(s32[1,6]{1,0:T(1,128)} %param.21) | copy-start | bytes 76
  128.3 3.3 %copy-start.23 = (s32[32]{0:T(128)S(1)}, s32[32]{0:T(128)}, u32[]{:S(2)}) copy-start(s32[32]{0:T(128)} %iota_add_fusion) | copy-start | bytes 388
  129.0 4.3 %copy-start.6 = (bf16[256,1024]{1,0:T(8,128)(2,1)S(1)}, bf16[256,1024]{1,0:T(8,128)(2,1)}, u32[]{:S(2)}) copy-start(bf16[256,1024]{1,0:T(8,128)(2,1)} %copy-done.5) | copy-start | bytes 1572868
  129.0 4.3 %copy-start.8 = (bf16[256,1024]{1,0:T(8,128)(2,1)S(1)}, bf16[256,1024]{1,0:T(8,128)(2,1)}, u32[]{:S(2)}) copy-start(bf16[256,1024]{1,0:T(8,128)(2,1)} %copy-done.7) | copy-start | bytes 1572868
  140.1 2.3 %copy-start.9 = (bf16[1,512,512]{1,2,0:T(8,128)(2,1)S(1)}, bf16[1,512,512]{1,2,0:T(8,128)(2,1)}, u32[]{:S(2)}) copy-start(bf16[1,512,512]{1,2,0:T(8,128)(2,1)} %get-tuple-element.8) | copy-start | bytes 1572868
  140.1 2.3 %copy-start.10 = (bf16[1,512,512]{1,2,0:T(8,128)(2,1)S(1)}, bf16[1,512,512]{1,2,0:T(8,128)(2,1)}, u32[]{:S(2)}) copy-start(bf16[1,512,512]{1,2,0:T(8,128)(2,1)} %get-tuple-element.7) | copy-start | bytes 1572868
  140.1 2.3 %copy-start.16 = (f32[512,4]{0,1:T(4,128)S(1)}, f32[512,4]{0,1:T(4,128)}, u32[]{:S(2)}) copy-start(f32[512,4]{0,1:T(4,128)} %fusion.69) | copy-start | bytes 24580
  140.1 2.3 %copy-start.18 = (f32[1,4,4,128]{3,1,2,0:T(4,128)S(1)}, f32[1,4,4,128]{3,1,2,0:T(4,128)}, u32[]{:S(2)}) copy-start(f32[1,4,4,128]{3,1,2,0:T(4,128)} %copy.83) | copy-start | bytes 24580
  142.4 2.9 %copy-start.17 = (f32[512,4]{0,1:T(4,128)S(1)}, f32[512,4]{0,1:T(4,128)}, u32[]{:S(2)}) copy-start(f32[512,4]{0,1:T(4,128)} %fusion.68) | copy-start | bytes 24580
  145.3 3.1 %copy-start.4 = (bf16[512,1024]{1,0:T(8,128)(2,1)S(1)}, bf16[512,1024]{1,0:T(8,128)(2,1)}, u32[]{:S(2)}) copy-start(bf16[512,1024]{1,0:T(8,128)(2,1)} %param.24) | copy-start | bytes 3145732
  148.4 5.0 %copy-start.2 = (bf16[256,1024]{1,0:T(8,128)(2,1)S(1)}, bf16[256,1024]{1,0:T(8,128)(2,1)}, u32[]{:S(2)}) copy-start(bf16[256,1024]{1,0:T(8,128)(2,1)} %param.13) | copy-start | bytes 1572868
  149.2 5.7 %copy-start.20 = (f32[1,1024]{1,0:T(1,128)S(1)}, f32[1,1024]{1,0:T(1,128)}, u32[]{:S(2)}) copy-start(f32[1,1024]{1,0:T(1,128)} %get-tuple-element.11) | copy-start | bytes 12292
  150.4 3.0 %collective-permute-start.2 = (f32[256,1024]{1,0:T(8,128)}, f32[256,1024]{1,0:T(8,128)}, u32[]{:S(2)}, u32[]{:S(2)}) collective-permute-start(f32[256,1024]{1,0:T(8,128)} %constant_dynamic-slice_fusion), channel_id=1, source_target_pairs={{0,1},{1,0},{2,3},{3,2},{4,5},{5,4},{6,7},{7,6},{8,9},{9,8},{10,11... | collective-permute-start | bytes 3145736 | tf_op jit(solution)/shard_map/ppermute | solution.py:20
  166.5 3.9 %copy-start.1 = (bf16[3,1024,512]{2,1,0:T(8,128)(2,1)S(1)}, bf16[3,1024,512]{2,1,0:T(8,128)(2,1)}, u32[]{:S(2)}) copy-start(bf16[3,1024,512]{2,1,0:T(8,128)(2,1)} %param.15) | copy-start | bytes 9437188
Sparse Core Ops, SparseCore 0:
  9.5 73.8 all-gather.2
  98.2 38.2 reduce-scatter.1
where the time goes:
time: 178 us; the launch traced here: 177 us
  waiting for transfers between devices  67 us (38%)
  matrix products  42.3 us (24%)
  local copies, waits for them, and re-layouts  22.9 us (13%)
  other arithmetic  20 us (11%)
  between operations  13.8 us (8%)
  blocking collectives  10.1 us (6%)
    all_gather x1, waiting for transfers between devices, on_device(): plane = lax.all_gather(caches, ('y', 'x'), axis=0, tiled=True)  63.2 us
    gather x2, local copies, waits for them, and re-layouts, on_device(): picked = plane[jnp.clip(local, 0, per_plane - 1)]  10.9 us
    all_gather x1, blocking collectives, on_device(): line_index = lax.all_gather(request_cache_index[0], 'z', axis=0)  10.1 us
    dot_general x2, matrix products, feed_half(): jnp.einsum('td,kdf->ktf', normed_two, weight[:2], preferred_element_type=...  8.73 us
    dot_general x2, matrix products, feed_half(): jnp.einsum('tf,df->td', hidden, weight[2], preferred_element_type=jnp.flo...  6.71 us
    unnamed x53, local copies, waits for them, and re-layouts  4.86 us
    sub x1, matrix products, on_device(): weights = jnp.exp(masked - peak)  4.67 us
    another operation x3, other arithmetic  4.54 us
  transfers between devices with their start and end apart: 6, of which 2 were waited for; matrix products, arithmetic and copies ran while one was open for 34% of the time, Pallas kernels for 0%

commit v1 on v0

--- a/solution.py
+++ b/solution.py
@@ -52,7 +52,9 @@
     scale = 1.0 / math.sqrt(head_size)
     ff_other = swap(feedforward_weight)
     down_other = swap(adapter_down_factor)
-    plane = lax.all_gather(caches, ("y", "x"), axis=0, tiled=True)
+    plane = jnp.concatenate(
+        lax.all_to_all(jnp.stack([caches] * lax.axis_size(("y", "x"))), ("y", "x"), 0, 0), axis=0
+    )
     per_plane = plane.shape[0]
     line_index = lax.all_gather(request_cache_index[0], "z", axis=0)
     local = line_index - lax.axis_index("z") * per_plane

time: 178 us -> 235 us (1.32)
  waiting for transfers between devices: 67 us -> 115 us
  starting transfers between devices: 1.23 us -> 10.2 us
    all_to_all x0 -> x1, waiting for transfers between devices: none -> 112 us  [on_device(): lax.all_to_all(jnp.stack([caches] * lax.axis_size(('y', 'x'))), ('y', 'x'...]
    all_gather x1 -> x0, waiting for transfers between devices: 63.2 us -> none  [on_device(): plane = lax.all_gather(caches, ('y', 'x'), axis=0, tiled=True)]
    all_to_all x0 -> x1, starting transfers between devices: none -> 7.77 us  [on_device(): lax.all_to_all(jnp.stack([caches] * lax.axis_size(('y', 'x'))), ('y', 'x'...]
    another operation x2 -> x3, local copies, waits for them, and re-layouts: 1.39 us -> 7.92 us  [the longest x1 6.54 us: on_device(): jnp.stack([caches] * lax.axis_size(('y', 'x')))]
    gather x2 -> x1, local copies, waits for them, and re-layouts: 10.9 us -> 6.19 us  [on_device(): picked = plane[jnp.clip(local, 0, per_plane - 1)]]
    unnamed x53 -> x57, local copies, waits for them, and re-layouts: 4.86 us -> 4.87 us
  transfers between devices with their start and end apart: 6 -> 6, of which waited for: 2 -> 2; matrix products, arithmetic and copies ran while one was open for 34% -> 25% of each run, Pallas kernels for 0% -> 0%
where the time goes in v1:
time: 235 us; the launch traced here: 234 us
  waiting for transfers between devices  115 us (49%)
  matrix products  42 us (18%)
  local copies, waits for them, and re-layouts  23.9 us (10%)
  other arithmetic  20 us (9%)
  between operations  13.8 us (6%)
  starting transfers between devices  10.2 us (4%)
  blocking collectives  9.33 us (4%)
    all_to_all x1, waiting for transfers between devices, on_device(): lax.all_to_all(jnp.stack([caches] * lax.axis_size(('y', 'x'))), ('y', 'x'...  112 us
    all_gather x1, blocking collectives, on_device(): line_index = lax.all_gather(request_cache_index[0], 'z', axis=0)  9.33 us
    dot_general x2, matrix products, feed_half(): jnp.einsum('td,kdf->ktf', normed_two, weight[:2], preferred_element_type=...  8.73 us
    all_to_all x1, starting transfers between devices, on_device(): lax.all_to_all(jnp.stack([caches] * lax.axis_size(('y', 'x'))), ('y', 'x'...  7.77 us
    dot_general x2, matrix products, feed_half(): jnp.einsum('tf,df->td', hidden, weight[2], preferred_element_type=jnp.flo...  6.71 us
    another operation x1, local copies, waits for them, and re-layouts, on_device(): jnp.stack([caches] * lax.axis_size(('y', 'x')))  6.54 us
    gather x1, local copies, waits for them, and re-layouts, on_device(): picked = plane[jnp.clip(local, 0, per_plane - 1)]  6.19 us
    unnamed x57, local copies, waits for them, and re-layouts  4.87 us
  transfers between devices with their start and end apart: 6, of which 2 were waited for; matrix products, arithmetic and copies ran while one was open for 25% of the time, Pallas kernels for 0%

profile of v1, /device:TPU:1, one launch (start us, length us, event | category | flops | bytes accessed | tf_op | source)
XLA Modules:
  0.0 234.0 jit_solution(13461446147499477883)
XLA Ops:
  6.5 6.5 %stack.2 = bf16[16,4,4,128,128]{4,3,2,1,0:T(8,128)(2,1)} broadcast(bf16[4,4,128,128]{3,2,1,0:T(8,128)(2,1)} %param.23), dimensions={1,2,3,4} | broadcast | bytes 8912896 | tf_op jit(solution)/shard_map/stack | solution.py:56
  13.1 7.8 %all-to-all-start = ((bf16[16,4,4,128,128]{4,3,2,1,0:T(8,128)(2,1)}), bf16[16,4,4,128,128]{4,3,2,1,0:T(8,128)(2,1)}, u32[]{:S(2)}, u32[]{:S(2)}) async-start(bf16[16,4,4,128,128]{4,3,2,1,0:T(8,128)(2,1)} %stack.2), calls=%async_computation | async-start | bytes 16777216 | tf_op jit(solution)/shard_map/all_to_all | solution.py:56
  20.9 9.3 %all-gather = s32[4,1,6]{2,1,0:T(1,128)S(1)} all-gather(s32[1,1,6]{2,1,0:T(1,128)S(1)} %bitcast.161), channel_id=1, replica_groups=mesh['z'=4,'y'=4,'x'=4,'col'=2] {'z'}, dimensions={0}, use_global_device_ids=true | all-gather | bytes 120 | tf_op jit(solution)/shard_map/all_gather | solution.py:59
  30.4 1.2 fusion.33
  32.2 111.8 %all-to-all-done = bf16[16,4,4,128,128]{4,3,2,1,0:T(8,128)(2,1)} async-done(((bf16[16,4,4,128,128]{4,3,2,1,0:T(8,128)(2,1)}), bf16[16,4,4,128,128]{4,3,2,1,0:T(8,128)(2,1)}, u32[]{:S(2)}, u32[]{:S(2)}) %all-to-all-start) | async-done | bytes 8388640 | tf_op jit(solution)/shard_map/all_to_all | solution.py:56
  144.0 6.2 %gather_fusion = bf16[24,4,128,128]{3,2,1,0:T(8,128)(2,1)} fusion(bf16[64,4,128,128]{3,2,1,0:T(8,128)(2,1)} %bitcast.23, s32[1024]{0:T(1024)S(1)} %pad_clamp_fusion), kind=kCustom, calls=%fused_computation | custom fusion | bytes 6291552 | tf_op jit(solution)/shard_map/gather | solution.py:62
  150.2 3.8 %broadcast_select_fusion = bf16[4,6,4,128,128]{4,3,2,1,0:T(8,128)(2,1)} fusion(bf16[4,6,4,128,128]{4,3,2,1,0:T(8,128)(2,1)} %bitcast.138, pred[4,6]{1,0:T(4,128)(4,1)S(1)} %bitcast.158), kind=kLoop, calls=%fused_computation.16 | loop fusion | flops 1572864 | bytes 6291480 | tf_op jit(solution)/shard_map/jit(_where)/select_n | solution.py:63
  154.0 2.0 fusion.35
  156.1 1.8 collective-permute-start
  157.9 2.8 %copy.48 = bf16[32,1024,16]{1,0,2:T(8,128)(2,1)} copy(bf16[32,1024,16]{1,2,0:T(8,128)(2,1)} %param.18) | data formatting | bytes 2097152 | tf_op args[5]
  163.6 2.5 %convolution_convert_fusion = bf16[6,16,512]{2,0,1:T(8,128)(2,1)S(1)} fusion(bf16[64,16,512]{2,1,0:T(8,128)(2,1)} %param.19, s32[6]{0:T(128)} %bitcast.153), kind=kOutput, calls=%fused_computation.48 | convolution fusion | flops 6340992 | bytes 1146904 | tf_op jit(solution)/shard_map/gq,qjl->gjl/dot_general | solution.py:96
  166.1 3.2 %fusion.73 = f32[6,1024,16]{1,0,2:T(8,128)} fusion(s32[32]{0:T(128)} %iota_add_fusion.1, s32[6]{0:T(128)} %bitcast.154, bf16[32,1024,16]{1,2,0:T(8,128)(2,1)} %param.18), kind=kOutput, calls=%fused_computation.111 | convolution fusion | flops 6291648 | bytes 1441944 | tf_op jit(solution)/shard_map/sa,adr->sdr/dot_general | solution.py:84
  169.3 1.5 broadcast_select_fusion.2
  171.7 1.1 convolution_bitcast_fusion.1
  174.1 1.3 reshape.282
  175.4 3.0 %reduce-window.18 = f32[4,4,128]{2,1,0:T(4,128)} reduce-window(f32[4,4,128]{2,1,0:T(4,128)} %reshape.282, f32[]{:T(128)} %constant.20.clone.1), window={size=1x1x128 pad=0_0x0_0x127_0}, to_apply=%region_7.8 | reduce-window | flops 260096 | bytes 16388 | tf_op jit(solution)/shard_map/reduce-window.1
  178.4 1.4 slice_reduce_fusion
  179.8 1.3 reduce-window.19
  181.9 3.1 %fusion.96 = (bf16[3,512,512]{1,2,0:T(8,128)(2,1)S(1)}, f32[3,512,512]{1,2,0:T(8,128)S(1)}) fusion(bf16[3,1024,512]{2,1,0:T(8,128)(2,1)S(1)} %copy-done, bf16[256,1024]{1,0:T(8,128)(2,1)} %copy-done.7, bf16[256,1024]{1,0:T(8,128)(2,1)} %copy-done.5), kind=kOutput, calls=%fused_computation.141 | convolution fusion | flops 1613496320 | bytes 8912896 | tf_op jit(solution)/shard_map/td,kdc->ktc/dot_general | solution.py:74
  187.2 1.1 fusion.94
  188.3 1.6 fusion.32
  192.1 4.7 %fusion.97 = (f32[4,512]{1,0:T(4,128)S(1)}, f32[4,512,512]{1,2,0:T(8,128)}) fusion(pred[512,512]{0,1:T(8,128)(4,1)S(1)} %fusion.43, bf16[512,4,128]{0,2,1:T(8,128)(2,1)S(1)} %add_convert_fusion, bf16[512,4,128]{0,2,1:T(8,128)(2,1)} %bitcast.144), kind=kOutput, calls=%fused_computation.142 | convolution fusion | flops 272630272 | bytes 5513216 | tf_op jit(solution)/shard_map/sub | solution.py:122
  196.9 2.3 fusion.1
  199.2 2.9 %multiply_reduce_fusion.1 = (f32[512,4]{0,1:T(4,128)S(1)}, f32[512,4,128]{0,2,1:T(8,128)}) fusion(f32[512,4,128]{0,2,1:T(8,128)S(1)} %fusion.1, f32[512,4]{0,1:T(4,128)S(1)} %copy-done.16, bf16[512,4,128]{0,2,1:T(8,128)(2,1)S(1)} %bitcast.142, f32[4,512]{1,0:T(4,128)S(1)} %bitcast.151, pred[512,512]{0,1:T(8,128)(4,1)S(1)} %fusion.43, ...), kind=kOutput, calls=%fused_computation.61 | convolution fusion | flops 543160320 | bytes 3956736 | tf_op jit(solution)/shard_map/hqk,khd->qhd/dot_general | solution.py:127
  202.1 3.1 %fusion.30 = bf16[512,4,128]{0,2,1:T(8,128)(2,1)S(1)} fusion(bf16[512,4,128]{0,2,1:T(8,128)(2,1)S(1)} %bitcast.143, f32[4,512,512]{1,2,0:T(8,128)} %get-tuple-element.16, f32[4,512]{1,0:T(4,128)S(1)} %get-tuple-element.15, f32[512,4,128]{0,2,1:T(8,128)} %get-tuple-element.18, f32[512,4]{0,1:T(4,128)S(1)} %add_rsqrt_fusion, f32[512,4]{0,1:T(4,128)S(1)} %copy-done.18), kind=kOutput, calls=%fused_computation.44 | convolution fusion | flops 271581184 | bytes 6316032 | tf_op jit(solution)/shard_map/hqk,khd->qhd/dot_general | solution.py:124
  206.0 1.2 constant_dynamic-slice_fusion
  207.2 3.0 %collective-permute-done.2 = f32[256,1024]{1,0:T(8,128)} collective-permute-done((f32[256,1024]{1,0:T(8,128)}, f32[256,1024]{1,0:T(8,128)}, u32[]{:S(2)}, u32[]{:S(2)}) %collective-permute-start.2) | collective-permute-done | bytes 1048608 | tf_op jit(solution)/shard_map/ppermute | solution.py:20
  210.2 1.5 fusion.37
  211.7 4.4 %fusion.6 = f32[2,256,1408]{2,1,0:T(8,128)S(1)} fusion(bf16[3,1024,1408]{2,1,0:T(8,128)(2,1)} %param.25, bf16[256,1024]{1,0:T(8,128)(2,1)S(1)} %get-tuple-element.6, f32[1024]{0:T(1024)S(1)} %bitcast.156, f32[256]{0:T(256)S(1)} %add_rsqrt_fusion.1), kind=kOutput, calls=%fused_computation.13 | convolution fusion | flops 1477443584 | bytes 9180160 | tf_op jit(solution)/shard_map/td,kdf->ktf/dot_general | solution.py:140
  216.1 2.9 %fusion.14 = f32[256,1024]{1,0:T(8,128)S(1)} fusion(bf16[3,1024,1408]{2,1,0:T(8,128)(2,1)} %param.25, f32[2,256,1408]{2,1,0:T(8,128)S(1)} %fusion.6), kind=kOutput, calls=%fused_computation.19 | convolution fusion | flops 740360192 | bytes 6815744 | tf_op jit(solution)/shard_map/tf,df->td/dot_general | solution.py:144
  219.0 4.4 %fusion.9 = f32[2,256,1408]{2,1,0:T(8,128)S(1)} fusion(bf16[3,1024,1408]{2,1,0:T(8,128)(2,1)} %collective-permute-done.3, bf16[256,1024]{1,0:T(8,128)(2,1)S(1)} %get-tuple-element.6, f32[1024]{0:T(1024)S(1)} %bitcast.157, f32[256]{0:T(256)S(1)} %add_rsqrt_fusion.1), kind=kOutput, calls=%fused_computation.14 | convolution fusion | flops 1477443584 | bytes 9180160 | tf_op jit(solution)/shard_map/td,kdf->ktf/dot_general | solution.py:140
  223.4 3.8 %fusion.31 = bf16[256,1024]{1,0:T(8,128)(2,1)} fusion(f32[256,1024]{1,0:T(8,128)S(1)} %fusion.14, bf16[3,1024,1408]{2,1,0:T(8,128)(2,1)} %collective-permute-done.3, bf16[256,1024]{1,0:T(8,128)(2,1)S(1)} %get-tuple-element.6, f32[2,256,1408]{2,1,0:T(8,128)S(1)} %fusion.9), kind=kOutput, calls=%fused_computation.45 | convolution fusion | flops 741408768 | bytes 7864320 | tf_op jit(solution)/shard_map/tf,df->td/dot_general | solution.py:144
  (99 shorter events, 11.8 us)
Async XLA Ops:
  6.5 175.4 %copy-start = (bf16[3,1024,512]{2,1,0:T(8,128)(2,1)S(1)}, bf16[3,1024,512]{2,1,0:T(8,128)(2,1)}, u32[]{:S(2)}) copy-start(bf16[3,1024,512]{2,1,0:T(8,128)(2,1)} %param.15) | copy-start | bytes 9437188
  13.1 7.8 %copy-start.25 = (s32[1,6]{1,0:T(1,128)S(1)}, s32[1,6]{1,0:T(1,128)}, u32[]{:S(2)}) copy-start(s32[1,6]{1,0:T(1,128)} %param.22) | copy-start | bytes 76
  13.1 18.5 %copy-start.17 = (f32[2,1024]{1,0:T(2,128)S(1)}, f32[2,1024]{1,0:T(2,128)}, u32[]{:S(2)}) copy-start(f32[2,1024]{1,0:T(2,128)} %param.14) | copy-start | bytes 24580
  13.1 130.9 %all-to-all-start = ((bf16[16,4,4,128,128]{4,3,2,1,0:T(8,128)(2,1)}), bf16[16,4,4,128,128]{4,3,2,1,0:T(8,128)(2,1)}, u32[]{:S(2)}, u32[]{:S(2)}) async-start(bf16[16,4,4,128,128]{4,3,2,1,0:T(8,128)(2,1)} %stack.2), calls=%async_computation | async-start | bytes 16777216 | tf_op jit(solution)/shard_map/all_to_all | solution.py:56
  20.9 176.0 %reduce-scatter.2.cloned.1.call-start = ((), (), s32[]{:S(2)}) async-start(), calls=%async_computation.2 | async-start | bytes 3932160 | tf_op jit(solution)/shard_map/reduce_scatter | solution.py:64
  32.2 121.8 %copy-start.12 = (f32[1,1024]{1,0:T(1,128)}, f32[1,1024]{1,0:T(1,128)S(1)}, u32[]{:S(2)}) copy-start(f32[1,1024]{1,0:T(1,128)S(1)} %get-tuple-element.12) | copy-start | bytes 12292
  154.0 7.2 %copy-start.26 = (s32[1,2,3]{2,1,0:T(2,128)S(1)}, s32[1,2,3]{2,1,0:T(2,128)}, u32[]{:S(2)}) copy-start(s32[1,2,3]{2,1,0:T(2,128)} %param.20) | copy-start | bytes 76
  154.0 2.0 copy-start.15
  156.1 13.3 %collective-permute-start = (bf16[256,1024]{1,0:T(8,128)(2,1)}, bf16[256,1024]{1,0:T(8,128)(2,1)}, u32[]{:S(2)}, u32[]{:S(2)}) collective-permute-start(bf16[256,1024]{1,0:T(8,128)(2,1)} %fusion.35), channel_id=1, source_target_pairs={{0,1},{1,0},{2,3},{3,2},{4,5},{5,4},{6,7},{7,6},{8,9},{9,8},{10,11... | collective-permute-start | bytes 1572872 | tf_op jit(solution)/shard_map/ppermute | solution.py:20
  160.7 27.6 %collective-permute-start.1 = (bf16[32,1024,16]{1,0,2:T(8,128)(2,1)}, bf16[32,1024,16]{1,0,2:T(8,128)(2,1)}, u32[]{:S(2)}, u32[]{:S(2)}) collective-permute-start(bf16[32,1024,16]{1,0,2:T(8,128)(2,1)} %copy.48), channel_id=1, source_target_pairs={{0,1},{1,0},{2,3},{3,2},{4,5},{5,4},{6,7},{7,6},{8,9},{9,8},{10,11... | collective-permute-start | bytes 3145736 | tf_op jit(solution)/shard_map/ppermute | solution.py:20
  160.7 58.3 %collective-permute-start.3 = (bf16[3,1024,1408]{2,1,0:T(8,128)(2,1)}, bf16[3,1024,1408]{2,1,0:T(8,128)(2,1)}, u32[]{:S(2)}, u32[]{:S(2)}) collective-permute-start(bf16[3,1024,1408]{2,1,0:T(8,128)(2,1)} %param.25), channel_id=1, source_target_pairs={{0,1},{1,0},{2,3},{3,2},{4,5},{5,4},{6,7},{7,6},{8,9},{9,8},{10,11... | collective-permute-start | bytes 25952264 | tf_op jit(solution)/shard_map/ppermute | solution.py:20
  163.6 9.8 %copy-start.22 = (f32[4]{0:T(128)S(1)}, f32[4]{0:T(128)}, u32[]{:S(2)}) copy-start(f32[4]{0:T(128)} %param.17) | copy-start | bytes 52
  170.9 0.8 copy-start.5
  170.9 1.9 copy-start.7
  181.9 3.1 %copy-start.14 = (f32[2,512,4]{1,2,0:T(4,128)S(1)}, f32[2,512,4]{1,2,0:T(4,128)}, u32[]{:S(2)}) copy-start(f32[2,512,4]{1,2,0:T(4,128)} %copy-done.13) | copy-start | bytes 49156
  181.9 3.1 %copy-start.23 = (f32[4]{0:T(128)S(1)}, f32[4]{0:T(128)}, u32[]{:S(2)}) copy-start(f32[4]{0:T(128)} %param.17) | copy-start | bytes 52
  181.9 3.9 %copy-start.11 = (f32[6,512]{1,0:T(8,128)S(1)}, f32[6,512]{1,0:T(8,128)}, u32[]{:S(2)}) copy-start(f32[6,512]{1,0:T(8,128)} %fusion.61) | copy-start | bytes 36868
  185.0 3.3 %copy-start.3 = (f32[6,1024,16]{1,0,2:T(8,128)S(1)}, f32[6,1024,16]{1,0,2:T(8,128)}, u32[]{:S(2)}) copy-start(f32[6,1024,16]{1,0,2:T(8,128)} %fusion.73) | copy-start | bytes 1179652
  185.0 3.3 %copy-start.20 = (s32[1,6]{1,0:T(1,128)S(1)}, s32[1,6]{1,0:T(1,128)}, u32[]{:S(2)}) copy-start(s32[1,6]{1,0:T(1,128)} %param.21) | copy-start | bytes 76
  185.1 3.3 %copy-start.24 = (s32[32]{0:T(128)S(1)}, s32[32]{0:T(128)}, u32[]{:S(2)}) copy-start(s32[32]{0:T(128)} %iota_add_fusion) | copy-start | bytes 388
  185.8 4.2 %copy-start.6 = (bf16[256,1024]{1,0:T(8,128)(2,1)S(1)}, bf16[256,1024]{1,0:T(8,128)(2,1)}, u32[]{:S(2)}) copy-start(bf16[256,1024]{1,0:T(8,128)(2,1)} %copy-done.5) | copy-start | bytes 1572868
  185.8 4.2 %copy-start.8 = (bf16[256,1024]{1,0:T(8,128)(2,1)S(1)}, bf16[256,1024]{1,0:T(8,128)(2,1)}, u32[]{:S(2)}) copy-start(bf16[256,1024]{1,0:T(8,128)(2,1)} %copy-done.7) | copy-start | bytes 1572868
  196.8 2.3 %copy-start.9 = (bf16[1,512,512]{1,2,0:T(8,128)(2,1)S(1)}, bf16[1,512,512]{1,2,0:T(8,128)(2,1)}, u32[]{:S(2)}) copy-start(bf16[1,512,512]{1,2,0:T(8,128)(2,1)} %get-tuple-element.8) | copy-start | bytes 1572868
  196.8 2.4 %copy-start.10 = (bf16[1,512,512]{1,2,0:T(8,128)(2,1)S(1)}, bf16[1,512,512]{1,2,0:T(8,128)(2,1)}, u32[]{:S(2)}) copy-start(bf16[1,512,512]{1,2,0:T(8,128)(2,1)} %get-tuple-element.7) | copy-start | bytes 1572868
  196.8 2.4 %copy-start.16 = (f32[512,4]{0,1:T(4,128)S(1)}, f32[512,4]{0,1:T(4,128)}, u32[]{:S(2)}) copy-start(f32[512,4]{0,1:T(4,128)} %fusion.69) | copy-start | bytes 24580
  196.8 2.4 %copy-start.19 = (f32[1,4,4,128]{3,1,2,0:T(4,128)S(1)}, f32[1,4,4,128]{3,1,2,0:T(4,128)}, u32[]{:S(2)}) copy-start(f32[1,4,4,128]{3,1,2,0:T(4,128)} %copy.86) | copy-start | bytes 24580
  199.2 2.9 %copy-start.18 = (f32[512,4]{0,1:T(4,128)S(1)}, f32[512,4]{0,1:T(4,128)}, u32[]{:S(2)}) copy-start(f32[512,4]{0,1:T(4,128)} %fusion.68) | copy-start | bytes 24580
  202.1 3.1 %copy-start.4 = (bf16[512,1024]{1,0:T(8,128)(2,1)S(1)}, bf16[512,1024]{1,0:T(8,128)(2,1)}, u32[]{:S(2)}) copy-start(bf16[512,1024]{1,0:T(8,128)(2,1)} %param.24) | copy-start | bytes 3145732
  205.2 5.0 %copy-start.2 = (bf16[256,1024]{1,0:T(8,128)(2,1)S(1)}, bf16[256,1024]{1,0:T(8,128)(2,1)}, u32[]{:S(2)}) copy-start(bf16[256,1024]{1,0:T(8,128)(2,1)} %param.13) | copy-start | bytes 1572868
  206.0 5.7 %copy-start.21 = (f32[1,1024]{1,0:T(1,128)S(1)}, f32[1,1024]{1,0:T(1,128)}, u32[]{:S(2)}) copy-start(f32[1,1024]{1,0:T(1,128)} %get-tuple-element.11) | copy-start | bytes 12292
  207.2 3.0 %collective-permute-start.2 = (f32[256,1024]{1,0:T(8,128)}, f32[256,1024]{1,0:T(8,128)}, u32[]{:S(2)}, u32[]{:S(2)}) collective-permute-start(f32[256,1024]{1,0:T(8,128)} %constant_dynamic-slice_fusion), channel_id=1, source_target_pairs={{0,1},{1,0},{2,3},{3,2},{4,5},{5,4},{6,7},{7,6},{8,9},{9,8},{10,11... | collective-permute-start | bytes 3145736 | tf_op jit(solution)/shard_map/ppermute | solution.py:20
  223.3 3.9 %copy-start.1 = (bf16[3,1024,512]{2,1,0:T(8,128)(2,1)S(1)}, bf16[3,1024,512]{2,1,0:T(8,128)(2,1)}, u32[]{:S(2)}) copy-start(bf16[3,1024,512]{2,1,0:T(8,128)(2,1)} %param.15) | copy-start | bytes 9437188
  (1 other events, 0.6 us)
Sparse Core Ops, SparseCore 0:
  154.1 40.6 reduce-scatter.1
